TPU v7x, 256 devices: a whole 4x4x8 slice. The times are simulated.
256 devices in a mesh: tile: 16 (over z, core), tensor: 16 (over y, x).
Axes of the slice: x: 4, y: 4, z: 8, core: 2. Of those that a mesh axis runs over, the one named last changes fastest.
Arguments:
- image_hidden: bfloat16 [8, 32, 32, 3072], P(None, 'tile', 'tensor'), may hold values from -6 to 6
- text_hidden: bfloat16 [8, 512, 3072], P(None, ('tile', 'tensor')), may hold values from -6 to 6
- latents: float32 [8, 32, 2048], P(None, 'tile', 'tensor'), may hold values from -6 to 6
- step_index: int32 [8], replicated, may hold values from 0 to 27
- anchor: int32 [8, 2], replicated, may hold values from 0 to 63
- text_len: int32 [8], replicated, may hold values from 64 to 512
- mod_image: float32 [8, 3, 3072], replicated, may hold values from -3 to 3
- mod_text: float32 [8, 3, 3072], replicated, may hold values from -3 to 3
- mod_mlp: float32 [8, 3, 3072], replicated, may hold values from -3 to 3
- mod_final: float32 [8, 2, 3072], replicated, may hold values from -3 to 3
- qkv_image: bfloat16 [3072, 3, 2048], P(None, None, 'tensor'), may hold values from -0.109375 to 0.109375
- qkv_text: bfloat16 [3072, 3, 2048], P(None, None, 'tensor'), may hold values from -0.109375 to 0.109375
- proj_image: bfloat16 [2048, 3072], P('tensor'), may hold values from -0.125 to 0.125
- proj_text: bfloat16 [2048, 3072], P('tensor'), may hold values from -0.125 to 0.125
- qk_gain: float32 [2, 2, 128], replicated, may hold values from 0.5 to 10
- mlp_expand: bfloat16 [3072, 6144], P(None, 'tensor'), may hold values from -0.109375 to 0.109375
- mlp_reduce: bfloat16 [6144, 3072], P('tensor'), may hold values from -0.078125 to 0.078125
- final_weight: bfloat16 [3072, 64], replicated, may hold values from -0.109375 to 0.109375
Outputs:
- image_out: bfloat16 [8, 32, 32, 3072], P(None, 'tile', 'tensor')
- text_out: bfloat16 [8, 512, 3072], P(None, ('tile', 'tensor'))
- latents_ext: float32 [8, 64, 2048], P(None, 'tile', 'tensor')
Inputs may be any that keep to these rules, and one draw needn't show every extreme that they name: text_len gives each request's live text tokens; slots at or past it take no part as keys. step_index is a step of the 28-step plan.
All inputs are finite; a program needn't handle non-finite values.
Results may differ from a plain program's by a relative error of at most 0.0085.
The roundings to bfloat16 on the way count: a program that leaves them out, or rounds other values in their place, can miss the bound.
Values may be sent and summed in bfloat16 or wider, within the bound.
No kernel may reach another device: no remote copies, remote signals or barrier semaphores. Data moves between devices by JAX's collectives and lax.ppermute only.
A program may use at most 128 MiB of HBM per device.

v0:
```python
import math
import jax
import jax.numpy as jnp
from jax import lax
from jax.sharding import PartitionSpec as P

HEAD_DIM = 128
GRID = 32
NSTEPS = 28
norm_eps = 1e-06
time_shift = 3.0


def padded(value, sides, width):
    for axis, dim in sides:
        size, length = (lax.axis_size(axis), value.shape[dim])
        up = [(i, (i + 1) % size) for i in range(size - 1)]
        down = [(j, i) for i, j in up]
        last = lax.slice_in_dim(value, length - width, length, axis=dim)
        leading = lax.slice_in_dim(value, 0, width, axis=dim)
        before = lax.ppermute(last, axis, up)
        after = lax.ppermute(leading, axis, down)
        value = jnp.concatenate([before, value, after], axis=dim)
    return value


def layer_norm(values):
    average = jnp.mean(values, -1, keepdims=True)
    centred = values - average
    spread = jnp.mean(centred * centred, -1, keepdims=True)
    return centred * lax.rsqrt(spread + norm_eps)


def modulate(hidden, shift, stretch):
    normed = layer_norm(hidden.astype(jnp.float32))
    return ((1.0 + stretch) * normed + shift).astype(jnp.bfloat16)


def rope_tables(row_ids, col_ids):
    lane = jnp.arange(2 * 64, dtype=jnp.int32)
    pair_index = lane // 2
    row_rank = (pair_index - 8).astype(jnp.float32)
    col_rank = (pair_index - 36).astype(jnp.float32)
    log_base = math.log(10000.0)
    row_freq = jnp.where(
        (pair_index >= 8) & (pair_index < 36), jnp.exp(-2.0 * row_rank / 56.0 * log_base), 0.0
    )
    col_freq = jnp.where(pair_index >= 36, jnp.exp(-2.0 * col_rank / 56.0 * log_base), 0.0)
    angles = row_ids[..., None] * row_freq + col_ids[..., None] * col_freq
    sign_table = jnp.where(lane % 2 == 0, -1.0, 1.0).astype(jnp.float32)
    return (jnp.cos(angles), jnp.sin(angles) * sign_table)


def rotate(values, cos_table, sin_table):
    lane = lax.broadcasted_iota(jnp.int32, values.shape, values.ndim - 1)
    swapped = jnp.where(lane % 2 == 0, jnp.roll(values, -1, axis=-1), jnp.roll(values, 1, axis=-1))
    return values * cos_table + swapped * sin_table


def head_norm(projected, head_gain):
    squares = jnp.mean(projected * projected, -1, keepdims=True)
    return projected * lax.rsqrt(squares + norm_eps) * head_gain


def sigma_of(step_float):
    level = 1.0 - step_float / NSTEPS
    return time_shift * level / (1.0 + (time_shift - 1.0) * level)


def key_usable(text_len, key_count, text_tile, block_len):
    key_pos = jnp.arange(key_count, dtype=jnp.int32)
    owner_tile = key_pos // block_len
    offset = key_pos % block_len
    text_pos = owner_tile * text_tile + offset
    return jnp.logical_or(offset[None, :] >= text_tile, text_pos[None, :] < text_len[:, None])


def sum_over_tensor(term, owners, narrow):
    if not narrow:
        return lax.psum_scatter(term, "tensor", scatter_dimension=0, tiled=True)
    parts = term.astype(jnp.bfloat16).reshape((owners, -1) + term.shape[1:])
    parts = lax.all_to_all(parts, "tensor", 0, 0, tiled=True)
    return jnp.sum(parts.astype(jnp.float32), 0)


NARROW_SUMS = True


def per_device(
    image_hidden,
    text_hidden,
    latents,
    step_index,
    anchor,
    text_len,
    mod_image,
    mod_text,
    mod_mlp,
    mod_final,
    qkv_image,
    qkv_text,
    proj_image,
    proj_text,
    qk_gain,
    mlp_expand,
    mlp_reduce,
    final_weight,
):
    requests, tile_rows, tile_cols, model_width = image_hidden.shape
    local_cols = qkv_image.shape[2]
    local_heads = local_cols // HEAD_DIM
    owners = lax.axis_size("tensor")
    own_image = tile_rows * tile_cols
    own_text = text_hidden.shape[1]
    slots = own_image + own_text
    image_own = image_hidden.reshape(requests, own_image, model_width).transpose(1, 0, 2)
    text_own = text_hidden.transpose(1, 0, 2)
    image_mod_own = modulate(image_own, mod_image[None, :, 0, :], mod_image[None, :, 1, :])
    text_mod_own = modulate(text_own, mod_text[None, :, 0, :], mod_text[None, :, 1, :])
    image_count = owners * own_image
    text_tile = owners * own_text
    block_len = text_tile + image_count
    image_mod = lax.all_gather(image_mod_own, "tensor", axis=0, tiled=True).reshape(
        image_count * requests, model_width
    )
    text_mod = lax.all_to_all(
        jnp.broadcast_to(text_mod_own[None], (owners,) + text_mod_own.shape),
        "tensor",
        0,
        0,
        tiled=True,
    ).reshape(text_tile * requests, model_width)
    tile_index = lax.axis_index("tile")
    token_index = jnp.arange(image_count, dtype=jnp.int32)
    owner = token_index // own_image
    within = token_index % own_image
    row_ids = (anchor[None, :, 0] + tile_index * tile_rows + (within // tile_cols)[:, None]).astype(
        jnp.float32
    )
    col_ids = (anchor[None, :, 1] + (owner * tile_cols + within % tile_cols)[:, None]).astype(
        jnp.float32
    )
    cos_table, sin_table = rope_tables(row_ids.reshape(-1), col_ids.reshape(-1))
    cos_table = cos_table[:, None, :]
    sin_table = sin_table[:, None, :]
    image_qkv = jnp.dot(
        image_mod,
        qkv_image.reshape(model_width, 3 * local_cols),
        preferred_element_type=jnp.float32,
    ).reshape(image_count * requests, 3, local_heads, HEAD_DIM)
    text_qkv = jnp.dot(
        text_mod, qkv_text.reshape(model_width, 3 * local_cols), preferred_element_type=jnp.float32
    ).reshape(text_tile * requests, 3, local_heads, HEAD_DIM)
    token_shape = (block_len, requests, local_heads, HEAD_DIM)
    query = jnp.concatenate(
        [
            head_norm(text_qkv[:, 0], qk_gain[1, 0]).astype(jnp.bfloat16),
            rotate(head_norm(image_qkv[:, 0], qk_gain[0, 0]), cos_table, sin_table).astype(
                jnp.bfloat16
            ),
        ],
        0,
    ).reshape(token_shape)
    keys = jnp.concatenate(
        [
            head_norm(text_qkv[:, 1], qk_gain[1, 1]).astype(jnp.bfloat16),
            rotate(head_norm(image_qkv[:, 1], qk_gain[0, 1]), cos_table, sin_table).astype(
                jnp.bfloat16
            ),
        ],
        0,
    ).reshape(token_shape)
    values = (
        jnp.concatenate([text_qkv[:, 2], image_qkv[:, 2]], 0)
        .astype(jnp.bfloat16)
        .reshape(token_shape)
    )
    score_scale = 1.0 / math.sqrt(HEAD_DIM)
    tiles = lax.axis_size("tile")
    parts = tiles // requests
    part_len = block_len // parts
    keys_r = jnp.repeat(keys.transpose(1, 0, 2, 3), parts, axis=0)
    values_r = jnp.repeat(values.transpose(1, 0, 2, 3), parts, axis=0)
    query_r = query.transpose(1, 0, 2, 3).reshape(tiles, part_len, local_heads, HEAD_DIM)
    outgoing = jnp.concatenate([keys_r, values_r, query_r], 1)
    incoming = lax.all_to_all(outgoing, "tile", 0, 0, tiled=True)
    keys_all = incoming[:, :block_len].reshape(tiles * block_len, local_heads, HEAD_DIM)
    values_all = incoming[:, block_len : 2 * block_len].reshape(
        tiles * block_len, local_heads, HEAD_DIM
    )
    query_mine = incoming[:, 2 * block_len :].reshape(tiles * part_len, local_heads, HEAD_DIM)
    my_request = tile_index // parts
    usable = key_usable(text_len[my_request][None], keys_all.shape[0], text_tile, block_len)[0][
        None, None, :
    ]
    scores = (
        jnp.einsum("qhd,khd->hqk", query_mine, keys_all, preferred_element_type=jnp.float32)
        * score_scale
    )
    row_top = jnp.max(jnp.where(usable, scores, -jnp.inf), -1, keepdims=True)
    weights_raw = jnp.where(usable, jnp.exp(scores - row_top), 0.0)
    weight_sum = jnp.sum(weights_raw, -1, keepdims=True)
    accum = jnp.einsum(
        "hqk,khd->hqd",
        weights_raw.astype(jnp.bfloat16),
        values_all,
        preferred_element_type=jnp.float32,
    )
    attended_mine = (
        (accum / weight_sum)
        .astype(jnp.bfloat16)
        .transpose(1, 0, 2)
        .reshape(tiles, part_len, local_heads * HEAD_DIM)
    )
    returned = lax.all_to_all(attended_mine, "tile", 0, 0, tiled=True)
    attended = returned.reshape(requests, block_len, local_cols).transpose(1, 0, 2)
    text_att = attended[:text_tile].reshape(text_tile * requests, local_cols)
    image_att = attended[text_tile:].reshape(image_count * requests, local_cols)
    image_term = jnp.dot(image_att, proj_image, preferred_element_type=jnp.float32).reshape(
        image_count, requests, model_width
    )
    image_sum = sum_over_tensor(image_term, owners, NARROW_SUMS)
    text_term = jnp.dot(text_att, proj_text, preferred_element_type=jnp.float32).reshape(
        text_tile, requests, model_width
    )
    after_image = (image_sum[0, 0, 0] * 0.0).astype(text_term.dtype)
    text_sum = sum_over_tensor(text_term + after_image, owners, NARROW_SUMS)
    image_mid = (image_own.astype(jnp.float32) + mod_image[None, :, 2, :] * image_sum).astype(
        jnp.bfloat16
    )
    mlp_mod = modulate(image_mid, mod_mlp[None, :, 0, :], mod_mlp[None, :, 1, :])
    piece = lax.all_gather(mlp_mod, "tensor", axis=0, tiled=True)
    grown = jnp.dot(piece.reshape(-1, model_width), mlp_expand, preferred_element_type=jnp.float32)
    activated = jax.nn.gelu(grown, approximate=True).astype(jnp.bfloat16)
    text_out = (text_own.astype(jnp.float32) + mod_text[None, :, 2, :] * text_sum).astype(
        jnp.bfloat16
    )
    mlp_term = jnp.dot(activated, mlp_reduce, preferred_element_type=jnp.float32).reshape(
        image_count, requests, model_width
    )
    mlp_sum = sum_over_tensor(mlp_term, owners, NARROW_SUMS)
    image_out = (image_mid.astype(jnp.float32) + mod_mlp[None, :, 2, :] * mlp_sum).astype(
        jnp.bfloat16
    )
    final_in = modulate(image_out, mod_final[None, :, 0, :], mod_final[None, :, 1, :])
    velocity = jnp.dot(
        final_in.reshape(own_image * requests, model_width),
        final_weight,
        preferred_element_type=jnp.float32,
    ).reshape(own_image, requests, final_weight.shape[1])
    velocity = velocity.transpose(1, 0, 2).reshape(
        requests, tile_rows, tile_cols * final_weight.shape[1]
    )
    step_float = step_index.astype(jnp.float32)
    time_delta = sigma_of(step_float + 1.0) - sigma_of(step_float)
    latents_next = latents + time_delta[:, None, None] * velocity
    latents_ext = padded(latents_next, (("tile", 1),), 1)
    image_out = image_out.transpose(1, 0, 2).reshape(requests, tile_rows, tile_cols, model_width)
    return (image_out, text_out.transpose(1, 0, 2), latents_ext)


def solution(mesh):
    return jax.shard_map(
        per_device,
        mesh=mesh,
        in_specs=(
            P(None, "tile", "tensor", None),
            P(None, ("tile", "tensor"), None),
            P(None, "tile", "tensor"),
            P(),
            P(),
            P(),
            P(),
            P(),
            P(),
            P(),
            P(None, None, "tensor"),
            P(None, None, "tensor"),
            P("tensor", None),
            P("tensor", None),
            P(),
            P(None, "tensor"),
            P("tensor", None),
            P(),
        ),
        out_specs=(
            P(None, "tile", "tensor", None),
            P(None, ("tile", "tensor"), None),
            P(None, "tile", "tensor"),
        ),
        check_vma=False,
    )
```

profile of v0, /device:TPU:97, one launch (start us, length us, event | category | flops | bytes accessed | tf_op | source)
XLA Modules:
  0.0 343.5 jit_solution(16405498130412113823)
XLA Ops:
  7.2 1.1 copy.54
  8.7 1.0 slice_bitcast_fusion.9
  9.7 0.8 add_convert_fusion.1
  10.6 1.0 fusion.66
  12.6 1.3 broadcast_in_dim.42
  13.9 6.8 %all-to-all-start = ((bf16[16,2,8,3072]{3,2,1,0:T(8,128)(2,1)}), bf16[16,2,8,3072]{3,2,1,0:T(8,128)(2,1)}, u32[]{:S(2)}, u32[]{:S(2)}) async-start(bf16[16,2,8,3072]{3,2,1,0:T(8,128)(2,1)} %broadcast_in_dim.42), calls=%async_computation | async-start | bytes 3145728 | tf_op jit(solution)/shard_map/all_to_all | solution.py:126
  20.7 4.3 %copy.57 = bf16[3072,3,128]{0,2,1:T(8,128)(2,1)} copy(bf16[3072,3,128]{2,0,1:T(8,128)(2,1)} %param.28) | data formatting | bytes 4718592 | tf_op args[10]
  25.3 4.3 %copy.56 = bf16[3072,3,128]{0,2,1:T(8,128)(2,1)} copy(bf16[3072,3,128]{2,0,1:T(8,128)(2,1)} %param.29) | data formatting | bytes 4718592 | tf_op args[11]
  31.9 14.3 %all-to-all-done = bf16[16,2,8,3072]{3,2,1,0:T(8,128)(2,1)} async-done(((bf16[16,2,8,3072]{3,2,1,0:T(8,128)(2,1)}), bf16[16,2,8,3072]{3,2,1,0:T(8,128)(2,1)}, u32[]{:S(2)}, u32[]{:S(2)}) %all-to-all-start) | async-done | bytes 1572896 | tf_op jit(solution)/shard_map/all_to_all | solution.py:126
  46.2 3.1 fusion.13
  49.8 0.7 copy.65
  50.5 0.7 copy.62
  51.3 24.4 %all-gather.3.cloned.1.call-done = bf16[64,8,3072]{2,1,0:T(8,128)(2,1)} async-done(((bf16[4,8,3072]{2,1,0:T(8,128)(2,1)}), bf16[64,8,3072]{2,1,0:T(8,128)(2,1)}) %all-gather.3.cloned.1.call-update) | async-done | bytes 3145744 | tf_op jit(solution)/shard_map/all_gather | solution.py:123
  75.7 4.0 %fusion.3 = f32[512,3,128]{0,2,1:T(8,128)S(1)} fusion(bf16[64,8,3072]{2,1,0:T(8,128)(2,1)} %all-gather.3.cloned.1.call-done, bf16[3072,3,128]{0,2,1:T(8,128)(2,1)} %copy.57), kind=kOutput, calls=%fused_computation.10 | convolution fusion | flops 1207959552 | bytes 6291456 | tf_op jit(solution)/shard_map/dot_general | solution.py:146
  80.9 2.1 fusion.60
  83.2 0.9 pad_maximum_fusion.3
  85.0 0.9 pad_maximum_fusion.2
  86.3 2.0 pad_maximum_fusion
  88.3 7.9 %all-to-all-start.1 = ((bf16[16,240,1,128]{3,1,2,0:T(8,128)(2,1)}), bf16[16,240,1,128]{3,1,2,0:T(8,128)(2,1)}, u32[]{:S(2)}, u32[]{:S(2)}) async-start(bf16[16,240,1,128]{3,1,2,0:T(8,128)(2,1)} %pad_maximum_fusion), calls=%async_computation.1 | async-start | bytes 1966080 | tf_op jit(solution)/shard_map/all_to_all | solution.py:186
  97.5 23.7 %all-to-all-done.1 = bf16[16,240,1,128]{3,1,2,0:T(8,128)(2,1)} async-done(((bf16[16,240,1,128]{3,1,2,0:T(8,128)(2,1)}), bf16[16,240,1,128]{3,1,2,0:T(8,128)(2,1)}, u32[]{:S(2)}, u32[]{:S(2)}) %all-to-all-start.1) | async-done | bytes 983072 | tf_op jit(solution)/shard_map/all_to_all | solution.py:186
  121.1 1.2 fusion.105
  122.3 0.9 slice.176
  123.2 0.9 select_reduce_fusion
  124.1 1.1 fusion.1
  125.2 0.9 fusion.19
  126.1 13.0 %all_to_all.30 = bf16[16,48,128]{2,1,0:T(8,128)(2,1)S(1)} all-to-all(bf16[16,48,128]{2,1,0:T(8,128)(2,1)S(1)} %bitcast.211), channel_id=1, replica_groups=mesh['tile'=16,'tensor'=16] {'tile'}, dimensions={0} | all-to-all | bytes 393216 | tf_op jit(solution)/shard_map/all_to_all | solution.py:215
  139.8 2.6 convolution_convert_fusion
  142.5 4.6 %all-to-all-start.3 = ((bf16[16,4,8,3072]{3,2,1,0:T(8,128)(2,1)}), bf16[16,4,8,3072]{3,2,1,0:T(8,128)(2,1)}, u32[]{:S(2)}, u32[]{:S(2)}) async-start(bf16[16,4,8,3072]{3,2,1,0:T(8,128)(2,1)} %bitcast.191), calls=%async_computation.3 | async-start | bytes 6291456 | tf_op jit(solution)/shard_map/all_to_all | solution.py:82
  148.0 46.9 %all-to-all-done.3 = bf16[16,4,8,3072]{3,2,1,0:T(8,128)(2,1)} async-done(((bf16[16,4,8,3072]{3,2,1,0:T(8,128)(2,1)}), bf16[16,4,8,3072]{3,2,1,0:T(8,128)(2,1)}, u32[]{:S(2)}, u32[]{:S(2)}) %all-to-all-start.3) | async-done | bytes 3145760 | tf_op jit(solution)/shard_map/all_to_all | solution.py:82
  194.9 2.5 convert_reduce_fusion.1
  197.9 0.8 fusion.45
  199.9 3.0 fusion
  202.9 4.4 %all-to-all-start.5 = ((bf16[16,2,8,3072]{3,2,1,0:T(8,128)(2,1)}), bf16[16,2,8,3072]{3,2,1,0:T(8,128)(2,1)}, u32[]{:S(2)}, u32[]{:S(2)}) async-start(bf16[16,2,8,3072]{3,2,1,0:T(8,128)(2,1)} %bitcast.192), calls=%async_computation.5 | async-start | bytes 3145728 | tf_op jit(solution)/shard_map/all_to_all | solution.py:82
  207.3 52.4 %all-gather.5.cloned.1.call-done = bf16[64,8,3072]{2,1,0:T(8,128)(2,1)} async-done(((bf16[4,8,3072]{2,1,0:T(8,128)(2,1)}), bf16[64,8,3072]{2,1,0:T(8,128)(2,1)}) %all-gather.5.cloned.1.call-update) | async-done | bytes 3145744 | tf_op jit(solution)/shard_map/all_gather | solution.py:232
  259.7 7.8 %convolution_convert_fusion.1 = bf16[512,3072]{1,0:T(8,128)(2,1)} fusion(bf16[384,3072]{1,0:T(8,128)(2,1)S(1)} %copy-done, bf16[3072,384]{1,0:T(8,128)(2,1)} %param.33, bf16[64,8,3072]{2,1,0:T(8,128)(2,1)} %all-gather.5.cloned.1.call-done), kind=kOutput, calls=%fused_computation.5 | convolution fusion | flops 2419261440 | bytes 11010048 | tf_op jit(solution)/shard_map/dot_general | solution.py:238
  267.5 4.6 %all-to-all-start.4 = ((bf16[16,4,8,3072]{3,2,1,0:T(8,128)(2,1)}), bf16[16,4,8,3072]{3,2,1,0:T(8,128)(2,1)}, u32[]{:S(2)}, u32[]{:S(2)}) async-start(bf16[16,4,8,3072]{3,2,1,0:T(8,128)(2,1)} %bitcast.193), calls=%async_computation.4 | async-start | bytes 6291456 | tf_op jit(solution)/shard_map/all_to_all | solution.py:82
  272.2 1.2 fusion.110
  274.1 1.6 convert_reduce_fusion.2
  275.8 0.7 copy.74
  276.6 41.8 %all-to-all-done.4 = bf16[16,4,8,3072]{3,2,1,0:T(8,128)(2,1)} async-done(((bf16[16,4,8,3072]{3,2,1,0:T(8,128)(2,1)}), bf16[16,4,8,3072]{3,2,1,0:T(8,128)(2,1)}, u32[]{:S(2)}, u32[]{:S(2)}) %all-to-all-start.4) | async-done | bytes 3145760 | tf_op jit(solution)/shard_map/all_to_all | solution.py:82
  318.4 2.5 convert_reduce_fusion
  320.9 1.0 convert_reduce_fusion.4
  322.2 1.3 convolution_bitcast_fusion
  323.7 6.2 %collective-permute-start = (f32[8,1,128]{2,1,0:T(1,128)S(1)}, f32[8,1,128]{2,1,0:T(1,128)S(1)}, u32[]{:S(2)}, u32[]{:S(2)}) collective-permute-start(f32[8,1,128]{2,1,0:T(1,128)S(1)} %get-tuple-element.33), channel_id=1, source_target_pairs={{0,16},{16,32},{32,48},{48,64},{64,80},{80,96},{96,112},{112,128},... | collective-permute-start | bytes 12296 | tf_op jit(solution)/shard_map/ppermute | solution.py:21
  329.9 1.9 collective-permute-start.1
  331.9 1.1 fusion.52
  332.9 0.9 copy.73
  333.8 2.2 collective-permute-done.1
  (116 shorter events, 12.3 us)
Async XLA Ops:
  7.2 252.6 %copy-start = (bf16[384,3072]{1,0:T(8,128)(2,1)S(1)}, bf16[384,3072]{1,0:T(8,128)(2,1)}, u32[]{:S(2)}) copy-start(bf16[384,3072]{1,0:T(8,128)(2,1)} %param.34) | copy-start | bytes 7077892
  7.2 4.4 %copy-start.2 = (bf16[8,2,3072]{2,1,0:T(2,128)(2,1)S(1)}, bf16[8,2,3072]{2,1,0:T(2,128)(2,1)}, u32[]{:S(2)}) copy-start(bf16[8,2,3072]{2,1,0:T(2,128)(2,1)} %param.19) | copy-start | bytes 294916
  7.2 4.6 %copy-start.10 = (f32[8,3,3072]{2,0,1:T(8,128)S(1)}, f32[8,3,3072]{2,0,1:T(8,128)}, u32[]{:S(2)}) copy-start(f32[8,3,3072]{2,0,1:T(8,128)} %param.25) | copy-start | bytes 884740
  7.2 68.5 %all-gather.3.cloned.1.call-start = ((), (), s32[]{:S(2)}) async-start(), calls=%async_computation.6 | async-start | bytes 3342336 | tf_op jit(solution)/shard_map/all_gather | solution.py:123
  13.9 32.3 %all-to-all-start = ((bf16[16,2,8,3072]{3,2,1,0:T(8,128)(2,1)}), bf16[16,2,8,3072]{3,2,1,0:T(8,128)(2,1)}, u32[]{:S(2)}, u32[]{:S(2)}) async-start(bf16[16,2,8,3072]{3,2,1,0:T(8,128)(2,1)} %broadcast_in_dim.42), calls=%async_computation | async-start | bytes 3145728 | tf_op jit(solution)/shard_map/all_to_all | solution.py:126
  20.7 4.3 %copy-start.14 = (s32[8,2]{0,1:T(2,128)S(1)}, s32[8,2]{0,1:T(2,128)}, u32[]{:S(2)}) copy-start(s32[8,2]{0,1:T(2,128)} %param.22) | copy-start | bytes 196
  25.0 6.9 %copy-start.13 = (f32[2,2,128]{2,1,0:T(2,128)S(1)}, f32[2,2,128]{2,1,0:T(2,128)}, u32[]{:S(2)}) copy-start(f32[2,2,128]{2,1,0:T(2,128)} %param.32) | copy-start | bytes 6148
  79.7 1.1 copy-start.15
  79.8 1.1 copy-start.16
  79.8 1.1 copy-start.17
  79.8 1.1 copy-start.18
  79.8 1.0 copy-start.19
  79.8 1.0 copy-start.20
  85.0 11.2 %copy-start.21 = (s32[8]{0:T(128)S(1)}, s32[8]{0:T(128)}, u32[]{:S(2)}) copy-start(s32[8]{0:T(128)} %param.23) | copy-start | bytes 100
  88.3 32.8 %all-to-all-start.1 = ((bf16[16,240,1,128]{3,1,2,0:T(8,128)(2,1)}), bf16[16,240,1,128]{3,1,2,0:T(8,128)(2,1)}, u32[]{:S(2)}, u32[]{:S(2)}) async-start(bf16[16,240,1,128]{3,1,2,0:T(8,128)(2,1)} %pad_maximum_fusion), calls=%async_computation.1 | async-start | bytes 1966080 | tf_op jit(solution)/shard_map/all_to_all | solution.py:186
  125.2 14.6 %copy-start.4 = (bf16[128,3072]{1,0:T(8,128)(2,1)S(1)}, bf16[128,3072]{1,0:T(8,128)(2,1)}, u32[]{:S(2)}) copy-start(bf16[128,3072]{1,0:T(8,128)(2,1)} %param.30) | copy-start | bytes 2359300
  139.1 0.7 copy-start.3
  142.5 4.9 %copy-start.11 = (f32[8,3,3072]{2,0,1:T(8,128)S(1)}, f32[8,3,3072]{2,0,1:T(8,128)}, u32[]{:S(2)}) copy-start(f32[8,3,3072]{2,0,1:T(8,128)} %param.26) | copy-start | bytes 884740
  142.5 52.5 %all-to-all-start.3 = ((bf16[16,4,8,3072]{3,2,1,0:T(8,128)(2,1)}), bf16[16,4,8,3072]{3,2,1,0:T(8,128)(2,1)}, u32[]{:S(2)}, u32[]{:S(2)}) async-start(bf16[16,4,8,3072]{3,2,1,0:T(8,128)(2,1)} %bitcast.191), calls=%async_computation.3 | async-start | bytes 6291456 | tf_op jit(solution)/shard_map/all_to_all | solution.py:82
  147.1 112.6 %all-gather.5.cloned.1.call-start = ((), (), s32[]{:S(2)}) async-start(), calls=%async_computation.7 | async-start | bytes 3342336 | tf_op jit(solution)/shard_map/all_gather | solution.py:232
  194.9 3.0 copy-start.5
  194.9 3.0 copy-start.6
  197.5 5.4 %copy-start.1 = (f32[4,8,3072]{2,1,0:T(8,128)}, f32[4,8,3072]{2,1,0:T(8,128)S(1)}, u32[]{:S(2)}) copy-start(f32[4,8,3072]{2,1,0:T(8,128)S(1)} %convert_reduce_fusion.1) | copy-start | bytes 1179652
  202.9 64.6 %all-to-all-start.5 = ((bf16[16,2,8,3072]{3,2,1,0:T(8,128)(2,1)}), bf16[16,2,8,3072]{3,2,1,0:T(8,128)(2,1)}, u32[]{:S(2)}, u32[]{:S(2)}) async-start(bf16[16,2,8,3072]{3,2,1,0:T(8,128)(2,1)} %bitcast.192), calls=%async_computation.5 | async-start | bytes 3145728 | tf_op jit(solution)/shard_map/all_to_all | solution.py:82
  267.5 4.7 %copy-start.22 = (s32[8]{0:T(128)S(1)}, s32[8]{0:T(128)}, u32[]{:S(2)}) copy-start(s32[8]{0:T(128)} %param.21) | copy-start | bytes 100
  267.5 8.2 %copy-start.9 = (f32[8,3072]{1,0:T(8,128)S(1)}, f32[8,3072]{1,0:T(8,128)}, u32[]{:S(2)}) copy-start(f32[8,3072]{1,0:T(8,128)} %get-tuple-element.14) | copy-start | bytes 294916
  267.5 50.9 %all-to-all-start.4 = ((bf16[16,4,8,3072]{3,2,1,0:T(8,128)(2,1)}), bf16[16,4,8,3072]{3,2,1,0:T(8,128)(2,1)}, u32[]{:S(2)}, u32[]{:S(2)}) async-start(bf16[16,4,8,3072]{3,2,1,0:T(8,128)(2,1)} %bitcast.193), calls=%async_computation.4 | async-start | bytes 6291456 | tf_op jit(solution)/shard_map/all_to_all | solution.py:82
  275.7 47.8 %copy-start.12 = (f32[8,2,128]{2,1,0:T(2,128)S(1)}, f32[8,2,128]{2,1,0:T(2,128)}, u32[]{:S(2)}) copy-start(f32[8,2,128]{2,1,0:T(2,128)} %param.20) | copy-start | bytes 24580
  275.8 46.4 %copy-start.7 = (f32[8,3072]{1,0:T(8,128)S(1)}, f32[8,3072]{1,0:T(8,128)}, u32[]{:S(2)}) copy-start(f32[8,3072]{1,0:T(8,128)} %get-tuple-element.55) | copy-start | bytes 294916
  318.4 3.8 %copy-start.8 = (f32[8,3072]{1,0:T(8,128)S(1)}, f32[8,3072]{1,0:T(8,128)}, u32[]{:S(2)}) copy-start(f32[8,3072]{1,0:T(8,128)} %get-tuple-element.56) | copy-start | bytes 294916
  323.7 10.1 %collective-permute-start = (f32[8,1,128]{2,1,0:T(1,128)S(1)}, f32[8,1,128]{2,1,0:T(1,128)S(1)}, u32[]{:S(2)}, u32[]{:S(2)}) collective-permute-start(f32[8,1,128]{2,1,0:T(1,128)S(1)} %get-tuple-element.33), channel_id=1, source_target_pairs={{0,16},{16,32},{32,48},{48,64},{64,80},{80,96},{96,112},{112,128},... | collective-permute-start | bytes 12296 | tf_op jit(solution)/shard_map/ppermute | solution.py:21
  329.9 6.1 %collective-permute-start.1 = (f32[8,1,128]{2,1,0:T(1,128)S(1)}, f32[8,1,128]{2,1,0:T(1,128)S(1)}, u32[]{:S(2)}, u32[]{:S(2)}) collective-permute-start(f32[8,1,128]{2,1,0:T(1,128)S(1)} %get-tuple-element.34), channel_id=1, source_target_pairs={{16,0},{32,16},{48,32},{64,48},{80,64},{96,80},{112,96},{128,112},... | collective-permute-start | bytes 12296 | tf_op jit(solution)/shard_map/ppermute | solution.py:22
Sparse Core Ops, SparseCore 0:
  11.0 64.6 all-gather.2
  198.8 60.8 all-gather.4
where the time goes:
time: 345 us; the launch traced here: 344 us
  waiting for transfers between devices  206 us (60%)
  starting transfers between devices  36.8 us (11%)
  other arithmetic  27.1 us (8%)
  matrix products  23.7 us (7%)
  local copies, waits for them, and re-layouts  21.9 us (6%)
  between operations  15.2 us (4%)
  blocking collectives  13 us (4%)
    all_to_all x3, waiting for transfers between devices, sum_over_tensor(): parts = lax.all_to_all(parts, 'tensor', 0, 0, tiled=True)  88.7 us
    all_gather x1, waiting for transfers between devices, per_device(): piece = lax.all_gather(mlp_mod, 'tensor', axis=0, tiled=True)  52.4 us
    all_gather x1, waiting for transfers between devices, per_device(): lax.all_gather(image_mod_own, 'tensor', axis=0, tiled=True)  24.4 us
    all_to_all x1, waiting for transfers between devices, per_device(): incoming = lax.all_to_all(outgoing, 'tile', 0, 0, tiled=True)  23.7 us
    all_to_all x1, waiting for transfers between devices, per_device(): lax.all_to_all(jnp.broadcast_to(text_mod_own[None], (owners,) + text_mod_...  14.3 us
    all_to_all x3, starting transfers between devices, sum_over_tensor(): parts = lax.all_to_all(parts, 'tensor', 0, 0, tiled=True)  13.6 us
    all_to_all x1, blocking collectives, per_device(): returned = lax.all_to_all(attended_mine, 'tile', 0, 0, tiled=True)  13 us
    unnamed x50, local copies, waits for them, and re-layouts  11 us
  transfers between devices with their start and end apart: 9, of which 7 were waited for; matrix products, arithmetic and copies ran while one was open for 11% of the time, Pallas kernels for 0%

commit v1 on v0

--- a/solution.py
+++ b/solution.py
@@ -120,9 +120,15 @@
     image_count = owners * own_image
     text_tile = owners * own_text
     block_len = text_tile + image_count
-    image_mod = lax.all_gather(image_mod_own, "tensor", axis=0, tiled=True).reshape(
-        image_count * requests, model_width
-    )
+    image_mod = jnp.concatenate(
+        lax.all_to_all(
+            jnp.stack([image_mod_own] * lax.axis_size("tensor"), axis=0),
+            axis_name="tensor",
+            concat_axis=0,
+            split_axis=0,
+        ),
+        axis=0,
+    ).reshape(image_count * requests, model_width)
     text_mod = lax.all_to_all(
         jnp.broadcast_to(text_mod_own[None], (owners,) + text_mod_own.shape),
         "tensor",

time: 345 us -> 362 us (1.049)
  waiting for transfers between devices: 206 us -> 216 us
  starting transfers between devices: 36.8 us -> 44.3 us
    all_to_all x0 -> x1, waiting for transfers between devices: none -> 28.6 us  [per_device(): lax.all_to_all(jnp.stack([image_mod_own] * lax.axis_size('tensor'), axis=...]
    all_gather x1 -> x0, waiting for transfers between devices: 24.4 us -> none  [per_device(): lax.all_gather(image_mod_own, 'tensor', axis=0, tiled=True)]
    all_to_all x1, waiting for transfers between devices: 14.3 us -> 21.4 us  [per_device(): lax.all_to_all(jnp.broadcast_to(text_mod_own[None], (owners,) + text_mod_...]
    all_to_all x0 -> x1, starting transfers between devices: none -> 4.61 us  [per_device(): lax.all_to_all(jnp.stack([image_mod_own] * lax.axis_size('tensor'), axis=...]
    unnamed x50 -> x38, local copies, waits for them, and re-layouts: 11 us -> 11 us
  transfers between devices with their start and end apart: 9 -> 9, of which waited for: 7 -> 7; matrix products, arithmetic and copies ran while one was open for 11% -> 10% of each run, Pallas kernels for 0% -> 0%
where the time goes in v1:
time: 362 us; the launch traced here: 361 us
  waiting for transfers between devices  216 us (60%)
  starting transfers between devices  44.3 us (12%)
  other arithmetic  26.2 us (7%)
  matrix products  23.7 us (7%)
  local copies, waits for them, and re-layouts  22.3 us (6%)
  between operations  15.2 us (4%)
  blocking collectives  13 us (4%)
    all_to_all x3, waiting for transfers between devices, sum_over_tensor(): parts = lax.all_to_all(parts, 'tensor', 0, 0, tiled=True)  89 us
    all_gather x1, waiting for transfers between devices, per_device(): piece = lax.all_gather(mlp_mod, 'tensor', axis=0, tiled=True)  51.4 us
    all_to_all x1, waiting for transfers between devices, per_device(): lax.all_to_all(jnp.stack([image_mod_own] * lax.axis_size('tensor'), axis=...  28.6 us
    all_to_all x1, waiting for transfers between devices, per_device(): incoming = lax.all_to_all(outgoing, 'tile', 0, 0, tiled=True)  23.7 us
    all_to_all x1, waiting for transfers between devices, per_device(): lax.all_to_all(jnp.broadcast_to(text_mod_own[None], (owners,) + text_mod_...  21.4 us
    all_to_all x3, starting transfers between devices, sum_over_tensor(): parts = lax.all_to_all(parts, 'tensor', 0, 0, tiled=True)  13.6 us
    all_to_all x1, blocking collectives, per_device(): returned = lax.all_to_all(attended_mine, 'tile', 0, 0, tiled=True)  13 us
    unnamed x38, local copies, waits for them, and re-layouts  11 us
  transfers between devices with their start and end apart: 9, of which 7 were waited for; matrix products, arithmetic and copies ran while one was open for 10% of the time, Pallas kernels for 0%

profile of v1, /device:TPU:97, one launch (start us, length us, event | category | flops | bytes accessed | tf_op | source)
XLA Modules:
  0.0 361.0 jit_solution(6165897578687986220)
XLA Ops:
  7.2 1.8 slice_bitcast_fusion.4
  9.0 1.0 fusion.65
  10.0 1.1 fusion.68
  11.1 1.0 fusion.71
  12.1 1.3 broadcast_in_dim.42
  13.4 6.8 %all-to-all-start = ((bf16[16,2,8,3072]{3,2,1,0:T(8,128)(2,1)}), bf16[16,2,8,3072]{3,2,1,0:T(8,128)(2,1)}, u32[]{:S(2)}, u32[]{:S(2)}) async-start(bf16[16,2,8,3072]{3,2,1,0:T(8,128)(2,1)} %broadcast_in_dim.42), calls=%async_computation | async-start | bytes 3145728 | tf_op jit(solution)/shard_map/all_to_all | solution.py:132
  20.7 1.0 slice_bitcast_fusion.9
  21.8 21.4 %all-to-all-done = bf16[16,2,8,3072]{3,2,1,0:T(8,128)(2,1)} async-done(((bf16[16,2,8,3072]{3,2,1,0:T(8,128)(2,1)}), bf16[16,2,8,3072]{3,2,1,0:T(8,128)(2,1)}, u32[]{:S(2)}, u32[]{:S(2)}) %all-to-all-start) | async-done | bytes 1572896 | tf_op jit(solution)/shard_map/all_to_all | solution.py:132
  43.2 2.1 stack.2
  45.2 4.6 %all-to-all-start.1 = ((bf16[16,4,8,3072]{3,2,1,0:T(8,128)(2,1)}), bf16[16,4,8,3072]{3,2,1,0:T(8,128)(2,1)}, u32[]{:S(2)}, u32[]{:S(2)}) async-start(bf16[16,4,8,3072]{3,2,1,0:T(8,128)(2,1)} %stack.2), calls=%async_computation.1 | async-start | bytes 6291456 | tf_op jit(solution)/shard_map/all_to_all | solution.py:124
  49.9 4.4 %copy.57 = bf16[3072,3,128]{0,2,1:T(8,128)(2,1)} copy(bf16[3072,3,128]{2,0,1:T(8,128)(2,1)} %param.28) | data formatting | bytes 4718592 | tf_op args[10]
  54.6 4.3 %copy.56 = bf16[3072,3,128]{0,2,1:T(8,128)(2,1)} copy(bf16[3072,3,128]{2,0,1:T(8,128)(2,1)} %param.29) | data formatting | bytes 4718592 | tf_op args[11]
  58.9 3.1 fusion.12
  62.5 0.7 copy.65
  63.4 28.6 %all-to-all-done.1 = bf16[16,4,8,3072]{3,2,1,0:T(8,128)(2,1)} async-done(((bf16[16,4,8,3072]{3,2,1,0:T(8,128)(2,1)}), bf16[16,4,8,3072]{3,2,1,0:T(8,128)(2,1)}, u32[]{:S(2)}, u32[]{:S(2)}) %all-to-all-start.1) | async-done | bytes 3145760 | tf_op jit(solution)/shard_map/all_to_all | solution.py:124
  92.0 4.0 %fusion.5 = f32[512,3,128]{0,2,1:T(8,128)S(1)} fusion(bf16[512,3072,1]{1,0,2:T(8,128)(2,1)} %bitcast.19, bf16[3072,3,128]{0,2,1:T(8,128)(2,1)} %copy.57), kind=kOutput, calls=%fused_computation.13 | convolution fusion | flops 1207959552 | bytes 6291456 | tf_op jit(solution)/shard_map/dot_general | solution.py:152
  97.0 2.1 fusion.59
  99.3 0.9 pad_maximum_fusion.3
  101.1 0.9 pad_maximum_fusion.2
  102.4 2.0 pad_maximum_fusion
  104.4 10.8 %all-to-all-start.2 = ((bf16[16,240,1,128]{3,1,2,0:T(8,128)(2,1)}), bf16[16,240,1,128]{3,1,2,0:T(8,128)(2,1)}, u32[]{:S(2)}, u32[]{:S(2)}) async-start(bf16[16,240,1,128]{3,1,2,0:T(8,128)(2,1)} %pad_maximum_fusion), calls=%async_computation.2 | async-start | bytes 1966080 | tf_op jit(solution)/shard_map/all_to_all | solution.py:192
  116.5 23.7 %all-to-all-done.2 = bf16[16,240,1,128]{3,1,2,0:T(8,128)(2,1)} async-done(((bf16[16,240,1,128]{3,1,2,0:T(8,128)(2,1)}), bf16[16,240,1,128]{3,1,2,0:T(8,128)(2,1)}, u32[]{:S(2)}, u32[]{:S(2)}) %all-to-all-start.2) | async-done | bytes 983072 | tf_op jit(solution)/shard_map/all_to_all | solution.py:192
  140.1 1.2 fusion.104
  141.3 0.9 slice.176
  142.3 0.9 select_reduce_fusion
  143.1 1.1 fusion.1
  144.2 0.9 fusion.18
  145.2 13.0 %all_to_all.35 = bf16[16,48,128]{2,1,0:T(8,128)(2,1)S(1)} all-to-all(bf16[16,48,128]{2,1,0:T(8,128)(2,1)S(1)} %bitcast.210), channel_id=1, replica_groups=mesh['tile'=16,'tensor'=16] {'tile'}, dimensions={0} | all-to-all | bytes 393216 | tf_op jit(solution)/shard_map/all_to_all | solution.py:221
  158.9 2.7 convolution_convert_fusion
  161.5 4.6 %all-to-all-start.4 = ((bf16[16,4,8,3072]{3,2,1,0:T(8,128)(2,1)}), bf16[16,4,8,3072]{3,2,1,0:T(8,128)(2,1)}, u32[]{:S(2)}, u32[]{:S(2)}) async-start(bf16[16,4,8,3072]{3,2,1,0:T(8,128)(2,1)} %bitcast.190), calls=%async_computation.4 | async-start | bytes 6291456 | tf_op jit(solution)/shard_map/all_to_all | solution.py:82
  167.1 47.2 %all-to-all-done.4 = bf16[16,4,8,3072]{3,2,1,0:T(8,128)(2,1)} async-done(((bf16[16,4,8,3072]{3,2,1,0:T(8,128)(2,1)}), bf16[16,4,8,3072]{3,2,1,0:T(8,128)(2,1)}, u32[]{:S(2)}, u32[]{:S(2)}) %all-to-all-start.4) | async-done | bytes 3145760 | tf_op jit(solution)/shard_map/all_to_all | solution.py:82
  214.3 2.5 convert_reduce_fusion.1
  217.3 0.8 fusion.44
  219.3 3.0 fusion
  222.3 4.4 %all-to-all-start.6 = ((bf16[16,2,8,3072]{3,2,1,0:T(8,128)(2,1)}), bf16[16,2,8,3072]{3,2,1,0:T(8,128)(2,1)}, u32[]{:S(2)}, u32[]{:S(2)}) async-start(bf16[16,2,8,3072]{3,2,1,0:T(8,128)(2,1)} %bitcast.191), calls=%async_computation.6 | async-start | bytes 3145728 | tf_op jit(solution)/shard_map/all_to_all | solution.py:82
  226.7 51.4 %all-gather.2.cloned.1.call-done = bf16[64,8,3072]{2,1,0:T(8,128)(2,1)} async-done(((bf16[4,8,3072]{2,1,0:T(8,128)(2,1)}), bf16[64,8,3072]{2,1,0:T(8,128)(2,1)}) %all-gather.2.cloned.1.call-update) | async-done | bytes 3145744 | tf_op jit(solution)/shard_map/all_gather | solution.py:238
  278.1 7.8 %convolution_convert_fusion.1 = bf16[512,3072]{1,0:T(8,128)(2,1)} fusion(bf16[384,3072]{1,0:T(8,128)(2,1)S(1)} %copy-done, bf16[3072,384]{1,0:T(8,128)(2,1)} %param.33, bf16[64,8,3072]{2,1,0:T(8,128)(2,1)} %all-gather.2.cloned.1.call-done), kind=kOutput, calls=%fused_computation.5 | convolution fusion | flops 2419261440 | bytes 11010048 | tf_op jit(solution)/shard_map/dot_general | solution.py:244
  285.9 4.6 %all-to-all-start.5 = ((bf16[16,4,8,3072]{3,2,1,0:T(8,128)(2,1)}), bf16[16,4,8,3072]{3,2,1,0:T(8,128)(2,1)}, u32[]{:S(2)}, u32[]{:S(2)}) async-start(bf16[16,4,8,3072]{3,2,1,0:T(8,128)(2,1)} %bitcast.192), calls=%async_computation.5 | async-start | bytes 6291456 | tf_op jit(solution)/shard_map/all_to_all | solution.py:82
  290.6 1.2 fusion.109
  292.5 1.6 convert_reduce_fusion.2
  294.9 41.8 %all-to-all-done.5 = bf16[16,4,8,3072]{3,2,1,0:T(8,128)(2,1)} async-done(((bf16[16,4,8,3072]{3,2,1,0:T(8,128)(2,1)}), bf16[16,4,8,3072]{3,2,1,0:T(8,128)(2,1)}, u32[]{:S(2)}, u32[]{:S(2)}) %all-to-all-start.5) | async-done | bytes 3145760 | tf_op jit(solution)/shard_map/all_to_all | solution.py:82
  336.7 2.5 convert_reduce_fusion
  339.7 1.3 convolution_bitcast_fusion
  341.2 6.2 %collective-permute-start = (f32[8,1,128]{2,1,0:T(1,128)S(1)}, f32[8,1,128]{2,1,0:T(1,128)S(1)}, u32[]{:S(2)}, u32[]{:S(2)}) collective-permute-start(f32[8,1,128]{2,1,0:T(1,128)S(1)} %get-tuple-element.33), channel_id=1, source_target_pairs={{0,16},{16,32},{32,48},{48,64},{64,80},{80,96},{96,112},{112,128},... | collective-permute-start | bytes 12296 | tf_op jit(solution)/shard_map/ppermute | solution.py:21
  347.4 1.9 collective-permute-start.1
  349.3 1.1 fusion.51
  350.4 0.9 copy.73
  351.3 2.3 collective-permute-done.1
  (104 shorter events, 10.2 us)
Async XLA Ops:
  7.2 270.9 %copy-start = (bf16[384,3072]{1,0:T(8,128)(2,1)S(1)}, bf16[384,3072]{1,0:T(8,128)(2,1)}, u32[]{:S(2)}) copy-start(bf16[384,3072]{1,0:T(8,128)(2,1)} %param.34) | copy-start | bytes 7077892
  7.2 13.1 %copy-start.11 = (bf16[8,2,2,3072]{3,2,1,0:T(2,128)(2,1)S(1)}, bf16[8,2,2,3072]{3,2,1,0:T(2,128)(2,1)}, u32[]{:S(2)}) copy-start(bf16[8,2,2,3072]{3,2,1,0:T(2,128)(2,1)} %param.18) | copy-start | bytes 589828
  13.4 29.7 %all-to-all-start = ((bf16[16,2,8,3072]{3,2,1,0:T(8,128)(2,1)}), bf16[16,2,8,3072]{3,2,1,0:T(8,128)(2,1)}, u32[]{:S(2)}, u32[]{:S(2)}) async-start(bf16[16,2,8,3072]{3,2,1,0:T(8,128)(2,1)} %broadcast_in_dim.42), calls=%async_computation | async-start | bytes 3145728 | tf_op jit(solution)/shard_map/all_to_all | solution.py:132
  45.2 46.7 %all-to-all-start.1 = ((bf16[16,4,8,3072]{3,2,1,0:T(8,128)(2,1)}), bf16[16,4,8,3072]{3,2,1,0:T(8,128)(2,1)}, u32[]{:S(2)}, u32[]{:S(2)}) async-start(bf16[16,4,8,3072]{3,2,1,0:T(8,128)(2,1)} %stack.2), calls=%async_computation.1 | async-start | bytes 6291456 | tf_op jit(solution)/shard_map/all_to_all | solution.py:124
  49.9 4.4 %copy-start.14 = (s32[8,2]{0,1:T(2,128)S(1)}, s32[8,2]{0,1:T(2,128)}, u32[]{:S(2)}) copy-start(s32[8,2]{0,1:T(2,128)} %param.22) | copy-start | bytes 196
  54.2 4.7 %copy-start.13 = (f32[2,2,128]{2,1,0:T(2,128)S(1)}, f32[2,2,128]{2,1,0:T(2,128)}, u32[]{:S(2)}) copy-start(f32[2,2,128]{2,1,0:T(2,128)} %param.32) | copy-start | bytes 6148
  101.1 14.1 %copy-start.15 = (s32[8]{0:T(128)S(1)}, s32[8]{0:T(128)}, u32[]{:S(2)}) copy-start(s32[8]{0:T(128)} %param.23) | copy-start | bytes 100
  104.4 35.8 %all-to-all-start.2 = ((bf16[16,240,1,128]{3,1,2,0:T(8,128)(2,1)}), bf16[16,240,1,128]{3,1,2,0:T(8,128)(2,1)}, u32[]{:S(2)}, u32[]{:S(2)}) async-start(bf16[16,240,1,128]{3,1,2,0:T(8,128)(2,1)} %pad_maximum_fusion), calls=%async_computation.2 | async-start | bytes 1966080 | tf_op jit(solution)/shard_map/all_to_all | solution.py:192
  144.2 14.6 %copy-start.4 = (bf16[128,3072]{1,0:T(8,128)(2,1)S(1)}, bf16[128,3072]{1,0:T(8,128)(2,1)}, u32[]{:S(2)}) copy-start(bf16[128,3072]{1,0:T(8,128)(2,1)} %param.30) | copy-start | bytes 2359300
  158.2 0.7 copy-start.3
  161.5 4.8 %copy-start.10 = (f32[8,3,3072]{2,0,1:T(8,128)S(1)}, f32[8,3,3072]{2,0,1:T(8,128)}, u32[]{:S(2)}) copy-start(f32[8,3,3072]{2,0,1:T(8,128)} %param.26) | copy-start | bytes 884740
  161.5 52.8 %all-to-all-start.4 = ((bf16[16,4,8,3072]{3,2,1,0:T(8,128)(2,1)}), bf16[16,4,8,3072]{3,2,1,0:T(8,128)(2,1)}, u32[]{:S(2)}, u32[]{:S(2)}) async-start(bf16[16,4,8,3072]{3,2,1,0:T(8,128)(2,1)} %bitcast.190), calls=%async_computation.4 | async-start | bytes 6291456 | tf_op jit(solution)/shard_map/all_to_all | solution.py:82
  166.1 111.9 %all-gather.2.cloned.1.call-start = ((), (), s32[]{:S(2)}) async-start(), calls=%async_computation.7 | async-start | bytes 3342336 | tf_op jit(solution)/shard_map/all_gather | solution.py:238
  214.3 3.0 copy-start.5
  214.3 3.0 copy-start.6
  216.9 5.4 %copy-start.1 = (f32[4,8,3072]{2,1,0:T(8,128)}, f32[4,8,3072]{2,1,0:T(8,128)S(1)}, u32[]{:S(2)}) copy-start(f32[4,8,3072]{2,1,0:T(8,128)S(1)} %convert_reduce_fusion.1) | copy-start | bytes 1179652
  222.3 63.6 %all-to-all-start.6 = ((bf16[16,2,8,3072]{3,2,1,0:T(8,128)(2,1)}), bf16[16,2,8,3072]{3,2,1,0:T(8,128)(2,1)}, u32[]{:S(2)}, u32[]{:S(2)}) async-start(bf16[16,2,8,3072]{3,2,1,0:T(8,128)(2,1)} %bitcast.191), calls=%async_computation.6 | async-start | bytes 3145728 | tf_op jit(solution)/shard_map/all_to_all | solution.py:82
  285.9 4.7 %copy-start.16 = (s32[8]{0:T(128)S(1)}, s32[8]{0:T(128)}, u32[]{:S(2)}) copy-start(s32[8]{0:T(128)} %param.21) | copy-start | bytes 100
  285.9 8.3 %copy-start.2 = (bf16[8,2,3072]{2,1,0:T(2,128)(2,1)S(1)}, bf16[8,2,3072]{2,1,0:T(2,128)(2,1)}, u32[]{:S(2)}) copy-start(bf16[8,2,3072]{2,1,0:T(2,128)(2,1)} %param.19) | copy-start | bytes 294916
  285.9 8.3 %copy-start.9 = (f32[8,3072]{1,0:T(8,128)S(1)}, f32[8,3072]{1,0:T(8,128)}, u32[]{:S(2)}) copy-start(f32[8,3072]{1,0:T(8,128)} %get-tuple-element.14) | copy-start | bytes 294916
  285.9 50.8 %all-to-all-start.5 = ((bf16[16,4,8,3072]{3,2,1,0:T(8,128)(2,1)}), bf16[16,4,8,3072]{3,2,1,0:T(8,128)(2,1)}, u32[]{:S(2)}, u32[]{:S(2)}) async-start(bf16[16,4,8,3072]{3,2,1,0:T(8,128)(2,1)} %bitcast.192), calls=%async_computation.5 | async-start | bytes 6291456 | tf_op jit(solution)/shard_map/all_to_all | solution.py:82
  294.1 46.9 %copy-start.12 = (f32[8,2,128]{2,1,0:T(2,128)S(1)}, f32[8,2,128]{2,1,0:T(2,128)}, u32[]{:S(2)}) copy-start(f32[8,2,128]{2,1,0:T(2,128)} %param.20) | copy-start | bytes 24580
  336.7 2.9 copy-start.7
  336.7 2.9 copy-start.8
  341.2 10.1 %collective-permute-start = (f32[8,1,128]{2,1,0:T(1,128)S(1)}, f32[8,1,128]{2,1,0:T(1,128)S(1)}, u32[]{:S(2)}, u32[]{:S(2)}) collective-permute-start(f32[8,1,128]{2,1,0:T(1,128)S(1)} %get-tuple-element.33), channel_id=1, source_target_pairs={{0,16},{16,32},{32,48},{48,64},{64,80},{80,96},{96,112},{112,128},... | collective-permute-start | bytes 12296 | tf_op jit(solution)/shard_map/ppermute | solution.py:21
  347.4 6.1 %collective-permute-start.1 = (f32[8,1,128]{2,1,0:T(1,128)S(1)}, f32[8,1,128]{2,1,0:T(1,128)S(1)}, u32[]{:S(2)}, u32[]{:S(2)}) collective-permute-start(f32[8,1,128]{2,1,0:T(1,128)S(1)} %get-tuple-element.34), channel_id=1, source_target_pairs={{16,0},{32,16},{48,32},{64,48},{80,64},{96,80},{112,96},{128,112},... | collective-permute-start | bytes 12296 | tf_op jit(solution)/shard_map/ppermute | solution.py:22
Sparse Core Ops, SparseCore 0:
  218.2 59.8 all-gather.1
